TPU v7x, 32 devices: a whole 2x2x4 slice. The times are simulated.
32 devices in a mesh: section: 2 (over x), fsdp: 16 (over z, y, core).
Axes of the slice: x: 2, y: 2, z: 4, core: 2. Of those that a mesh axis runs over, the one named last changes fastest.
Arguments:
- history: bfloat16 [4, 16, 32, 2048], P(None, 'fsdp'), may hold values from -6 to 6
- keymask: int32 [4, 16, 32], P(None, 'fsdp'), may hold values from 0 to 1, as said below
- codes: int32 [4, 16, 16, 2], P(None, 'fsdp'), may hold values from 0 to 15
- plan_table: bfloat16 [16, 2048], replicated, may hold values from -6 to 6
- query_weights: bfloat16 [2, 2048, 1024], P('section', 'fsdp'), may hold values from -0.125 to 0.125
- output_weights: bfloat16 [2, 1024, 2048], P('section', 'fsdp'), may hold values from -0.75 to 0.75
- gains: float32 [2, 2048], P('section'), may hold values from 0.5 to 1.5
- cotangent: bfloat16 [4, 16, 32, 2048], P(None, 'fsdp'), may hold values from -6 to 6
Outputs:
- section_grads: bfloat16 [2, 4, 16, 32, 2048], P('section', None, 'fsdp')
- gain_grads: float32 [2, 2048], P('section')
Inputs may be any that keep to these rules, and one draw needn't show every extreme that they name: `keymask`: in each series the ones form one run that ends at the last position and covers at least a quarter of the 32 positions.
All inputs are finite; a program needn't handle non-finite values.
Results may differ from a plain program's by a relative error of at most 0.014.
Values may be sent and summed in bfloat16 or wider, within the bound.
No kernel may reach another device: no remote copies, remote signals or barrier semaphores. Data moves between devices by JAX's collectives and lax.ppermute only.
A program may use at most 64 MiB of HBM per device.

v0:
```python
import math
import jax
import jax.numpy as jnp
from jax import lax
from jax.sharding import PartitionSpec as P

HEADS = 8
EPSILON = 1e-05


def shifted(array, axis, by):
    size = lax.axis_size(axis)
    pairs = [(i, i + by) for i in range(size) if 0 <= i + by < size]
    return lax.ppermute(array, axis, pairs)


def rms_scale(inputs, gain_vector):
    return (
        inputs
        * lax.rsqrt(jnp.mean(inputs * inputs, axis=-1, keepdims=True) + EPSILON)
        * gain_vector
    )


def attend_layer(section_input, source, key_mask, query_weight, output_weight, gain_vector):
    series_count, seq_length, model_width = section_input.shape
    half_width = model_width // 2
    head_dim = half_width // HEADS
    head_shape = (series_count, seq_length, HEADS, head_dim)
    input_wide = section_input.astype(jnp.float32)
    normed = rms_scale(input_wide, gain_vector)
    normed_source = rms_scale(source.astype(jnp.float32), gain_vector)
    normed_rows = normed.astype(jnp.bfloat16).reshape(series_count * seq_length, model_width)
    query_flat = jnp.dot(normed_rows, query_weight, preferred_element_type=jnp.float32)
    queries = query_flat.astype(jnp.bfloat16).reshape(head_shape)
    key_rows = normed_source[..., :half_width].astype(jnp.bfloat16).reshape(head_shape)
    value_rows = normed_source[..., half_width:].astype(jnp.bfloat16).reshape(head_shape)
    scores = jnp.einsum(
        "bqhd,bkhd->bhqk", queries, key_rows, preferred_element_type=jnp.float32
    ) / math.sqrt(head_dim)
    raised = jnp.exp(scores) * key_mask.astype(jnp.float32)[:, None, None, :]
    probs = (raised / jnp.sum(raised, axis=-1, keepdims=True)).astype(jnp.bfloat16)
    mixed = jnp.einsum("bhqk,bkhd->bqhd", probs, value_rows, preferred_element_type=jnp.float32)
    mixed = mixed.astype(jnp.bfloat16).reshape(series_count * seq_length, half_width)
    update = jnp.dot(mixed, output_weight, preferred_element_type=jnp.float32)
    return (input_wide + update.reshape(series_count, seq_length, model_width)).astype(jnp.bfloat16)


def pick_slot(stack, slot):
    return lax.dynamic_index_in_dim(stack, slot, 0, False)


def place_slot(stack, slot, update, keep):
    previous = pick_slot(stack, slot)
    return lax.dynamic_update_index_in_dim(stack, jnp.where(keep, update, previous), slot, 0)


def on_device(history, keymask, codes, plan_table, query_weights, output_weights, gains, cotangent):
    section_index = lax.axis_index("section")
    section_count = lax.axis_size("section")
    half_sections = section_count // 2
    micro_count, series_count, seq_length, model_width = history.shape
    gathered_query, gathered_output = (
        lax.all_gather(query_weights, "fsdp", axis=1, tiled=True),
        lax.all_gather(output_weights, "fsdp", axis=1, tiled=True),
    )
    query_weight = gathered_query[0]
    output_weight = gathered_output[0]
    gain_vector = gains[0]
    code_rows = codes.reshape(micro_count, series_count, seq_length)
    code_count = plan_table.shape[0]
    one_hot = (code_rows[..., None] == jnp.arange(code_count, dtype=jnp.int32)).astype(jnp.bfloat16)
    plan_tokens = jnp.einsum(
        "msln,nd->msld", one_hot, plan_table, preferred_element_type=jnp.float32
    ).astype(jnp.bfloat16)
    is_decoder = section_index >= half_sections
    zero_act = jnp.zeros((series_count, seq_length, model_width), jnp.bfloat16)
    zero_stack = jnp.zeros(history.shape, jnp.bfloat16)
    tick_count = micro_count + section_count - 1

    def forward_tick(tick_index, state_tuple):
        got_input, got_memory, inputs_buf, memory_buf = state_tuple
        micro_index = tick_index - section_index
        is_active = (micro_index >= 0) & (micro_index < micro_count)
        slot = jnp.clip(micro_index, 0, micro_count - 1)
        key_mask = pick_slot(keymask, slot)
        section_input = jnp.where(
            section_index == 0,
            pick_slot(history, slot),
            jnp.where(section_index == half_sections, pick_slot(plan_tokens, slot), got_input),
        )
        memory = got_memory
        source = jnp.where(is_decoder, memory, section_input)

        def run_layer():
            return attend_layer(
                section_input, source, key_mask, query_weight, output_weight, gain_vector
            )

        def skip_layer():
            return zero_act

        output = lax.cond(is_active, run_layer, skip_layer)
        inputs_buf = place_slot(inputs_buf, slot, section_input, is_active)
        memory_buf = place_slot(memory_buf, slot, memory, is_active & is_decoder)
        outgoing = jnp.where(
            section_index == half_sections - 1, output, jnp.where(is_decoder, memory, zero_act)
        )
        got_input, got_memory = shifted((output, outgoing), "section", 1)
        return (got_input, got_memory, inputs_buf, memory_buf)

    start_state = (zero_act, zero_act, zero_stack, zero_stack)
    _, _, inputs_buf, memory_buf = lax.fori_loop(0, tick_count, forward_tick, start_state)

    def backward_tick(tick_index, state_tuple):
        got_grad, got_memory_grad, grads_buf, gain_total = state_tuple
        micro_index = tick_index - (section_count - 1 - section_index)
        is_active = (micro_index >= 0) & (micro_index < micro_count)
        slot = jnp.clip(micro_index, 0, micro_count - 1)
        key_mask = pick_slot(keymask, slot)
        out_grad = jnp.where(
            section_index == section_count - 1, pick_slot(cotangent, slot), got_grad
        )
        section_input = pick_slot(inputs_buf, slot)
        memory = pick_slot(memory_buf, slot)

        def section_map(layer_input, layer_memory, layer_gain):
            layer_source = jnp.where(is_decoder, layer_memory, layer_input)
            return attend_layer(
                layer_input, layer_source, key_mask, query_weight, output_weight, layer_gain
            )

        def run_grads():
            _, pull = jax.vjp(section_map, section_input, memory, gain_vector)
            return pull(out_grad)

        def skip_grads():
            return (zero_act, zero_act, jnp.zeros_like(gain_vector))

        input_grad, memory_grad, gain_grad = lax.cond(is_active, run_grads, skip_grads)
        memory_sum = jnp.where(is_decoder, got_memory_grad + memory_grad, zero_act)
        send_main = jnp.where(section_index == half_sections, memory_sum, input_grad)
        send_side = jnp.where(is_decoder & (section_index != half_sections), memory_sum, zero_act)
        got_grad, got_memory_grad = shifted((send_main, send_side), "section", -1)
        grads_buf = place_slot(grads_buf, slot, input_grad, is_active)
        gain_total = gain_total + lax.psum(gain_grad, "fsdp")
        return (got_grad, got_memory_grad, grads_buf, gain_total)

    back_state = (zero_act, zero_act, zero_stack, jnp.zeros_like(gain_vector))
    _, _, grads_buf, gain_total = lax.fori_loop(0, tick_count, backward_tick, back_state)
    return (grads_buf[None], gain_total[None])


def solution(mesh):
    return jax.shard_map(
        on_device,
        mesh=mesh,
        in_specs=(
            P(None, "fsdp", None, None),
            P(None, "fsdp", None),
            P(None, "fsdp", None, None),
            P(),
            P("section", "fsdp", None),
            P("section", "fsdp", None),
            P("section", None),
            P(None, "fsdp", None, None),
        ),
        out_specs=(P("section", None, "fsdp", None, None), P("section", None)),
        check_vma=False,
    )
```

profile of v0, /device:TPU:0, one launch (start us, length us, event | category | flops | bytes accessed | tf_op | source)
XLA Modules:
  0.0 415.8 jit_solution(3246150808287306456)
XLA Ops:
  9.9 53.6 %all-gather.3.cloned.1.call-done = bf16[1,1024,2048]{2,1,0:T(8,128)(2,1)} async-done(((bf16[1,64,2048]{2,1,0:T(8,128)(2,1)}), bf16[1,1024,2048]{2,1,0:T(8,128)(2,1)}) %all-gather.3.cloned.1.call-update) | async-done | bytes 4194320 | tf_op jit(solution)/shard_map/all_gather | solution.py:65
  63.5 51.2 %all-gather.5.cloned.1.call-done = bf16[1,2048,1024]{2,1,0:T(8,128)(2,1)} async-done(((bf16[1,128,1024]{2,1,0:T(8,128)(2,1)}), bf16[1,2048,1024]{2,1,0:T(8,128)(2,1)}) %all-gather.5.cloned.1.call-update) | async-done | bytes 4194320 | tf_op jit(solution)/shard_map/all_gather | solution.py:64
  114.9 89.8 %while.42 = (s32[]{:T(128)}, bf16[1,32,2048]{2,1,0:T(8,128)(2,1)S(1)}, bf16[1,32,2048]{2,1,0:T(8,128)(2,1)S(1)}, bf16[4,1,32,2048]{3,2,1,0:T(8,128)(2,1)S(1)}, b...) while((s32[]{:T(128)}, ...), condition=%wide.region_6.7_spmd, body=%wide.region_0.6_spmd.sunk | while | flops 274366848 | bytes 14173985 | solution.py:113
  116.0 8.3 %conditional.5 = (bf16[1,32,2048]{2,1,0:T(8,128)(2,1)S(1)}) conditional(s32[]{:T(128)} %convert_element_type.398, () %tuple.120, (bf16[1,32,2048]{2,1,0:T(8,128)(2,1)S(1)}, pred[1,32,2048]{2,1,0:T(8,128)(4,1)S(1)}, bf16[1,32,2048]{2,1,0:T(8,128)(2,1)S(1)}, f32[1,2048]{1,0:T(1,128)}, bf16[2048,1024]{1,0:T(8,128)(2,1)}, ...), branch_computations={%region_1.1_spmd, %region_2.5_spmd} | conditional | flops 273973632 | bytes 10700172 | solution.py:103
  117.0 3.1 fusion.5
  127.0 4.8 %collective-permute-done.1 = bf16[1,32,2048]{2,1,0:T(8,128)(2,1)S(1)} collective-permute-done((bf16[1,32,2048]{2,1,0:T(8,128)(2,1)S(1)}, bf16[1,32,2048]{2,1,0:T(8,128)(2,1)S(1)}, u32[]{:S(2)}, u32[]{:S(2)}) %collective-permute-start.1) | collective-permute-done | bytes 131104 | tf_op jit(solution)/shard_map/while/body/eval_jaxpr/ppermute | solution.py:14
  132.9 8.3 %conditional.5 = (bf16[1,32,2048]{2,1,0:T(8,128)(2,1)S(1)}) conditional(s32[]{:T(128)} %convert_element_type.398, () %tuple.120, (bf16[1,32,2048]{2,1,0:T(8,128)(2,1)S(1)}, pred[1,32,2048]{2,1,0:T(8,128)(4,1)S(1)}, bf16[1,32,2048]{2,1,0:T(8,128)(2,1)S(1)}, f32[1,2048]{1,0:T(1,128)}, bf16[2048,1024]{1,0:T(8,128)(2,1)}, ...), branch_computations={%region_1.1_spmd, %region_2.5_spmd} | conditional | flops 273973632 | bytes 10700172 | solution.py:103
  134.0 3.1 fusion.5
  141.2 4.4 %collective-permute-start = (bf16[1,32,2048]{2,1,0:T(8,128)(2,1)S(1)}, bf16[1,32,2048]{2,1,0:T(8,128)(2,1)S(1)}, u32[]{:S(2)}, u32[]{:S(2)}) collective-permute-start(bf16[1,32,2048]{2,1,0:T(8,128)(2,1)S(1)} %get-tuple-element.1286), channel_id=1, source_target_pairs={{0,16},{1,17},{2,18},{3,19},{4,20},{5,21},{6,22},{7,23},{8,24},{9,... | collective-permute-start | bytes 393224 | tf_op jit(solution)/shard_map/while/body/eval_jaxpr/ppermute | solution.py:14
  147.0 4.0 collective-permute-done.1
  152.1 8.3 %conditional.5 = (bf16[1,32,2048]{2,1,0:T(8,128)(2,1)S(1)}) conditional(s32[]{:T(128)} %convert_element_type.398, () %tuple.120, (bf16[1,32,2048]{2,1,0:T(8,128)(2,1)S(1)}, pred[1,32,2048]{2,1,0:T(8,128)(4,1)S(1)}, bf16[1,32,2048]{2,1,0:T(8,128)(2,1)S(1)}, f32[1,2048]{1,0:T(1,128)}, bf16[2048,1024]{1,0:T(8,128)(2,1)}, ...), branch_computations={%region_1.1_spmd, %region_2.5_spmd} | conditional | flops 273973632 | bytes 10700172 | solution.py:103
  153.2 3.1 fusion.5
  160.4 4.4 %collective-permute-start = (bf16[1,32,2048]{2,1,0:T(8,128)(2,1)S(1)}, bf16[1,32,2048]{2,1,0:T(8,128)(2,1)S(1)}, u32[]{:S(2)}, u32[]{:S(2)}) collective-permute-start(bf16[1,32,2048]{2,1,0:T(8,128)(2,1)S(1)} %get-tuple-element.1286), channel_id=1, source_target_pairs={{0,16},{1,17},{2,18},{3,19},{4,20},{5,21},{6,22},{7,23},{8,24},{9,... | collective-permute-start | bytes 393224 | tf_op jit(solution)/shard_map/while/body/eval_jaxpr/ppermute | solution.py:14
  166.2 3.2 collective-permute-done.1
  170.5 8.3 %conditional.5 = (bf16[1,32,2048]{2,1,0:T(8,128)(2,1)S(1)}) conditional(s32[]{:T(128)} %convert_element_type.398, () %tuple.120, (bf16[1,32,2048]{2,1,0:T(8,128)(2,1)S(1)}, pred[1,32,2048]{2,1,0:T(8,128)(4,1)S(1)}, bf16[1,32,2048]{2,1,0:T(8,128)(2,1)S(1)}, f32[1,2048]{1,0:T(1,128)}, bf16[2048,1024]{1,0:T(8,128)(2,1)}, ...), branch_computations={%region_1.1_spmd, %region_2.5_spmd} | conditional | flops 273973632 | bytes 10700172 | solution.py:103
  171.5 3.1 fusion.5
  178.8 4.4 %collective-permute-start = (bf16[1,32,2048]{2,1,0:T(8,128)(2,1)S(1)}, bf16[1,32,2048]{2,1,0:T(8,128)(2,1)S(1)}, u32[]{:S(2)}, u32[]{:S(2)}) collective-permute-start(bf16[1,32,2048]{2,1,0:T(8,128)(2,1)S(1)} %get-tuple-element.1286), channel_id=1, source_target_pairs={{0,16},{1,17},{2,18},{3,19},{4,20},{5,21},{6,22},{7,23},{8,24},{9,... | collective-permute-start | bytes 393224 | tf_op jit(solution)/shard_map/while/body/eval_jaxpr/ppermute | solution.py:14
  188.2 12.6 %collective-permute-start = (bf16[1,32,2048]{2,1,0:T(8,128)(2,1)S(1)}, bf16[1,32,2048]{2,1,0:T(8,128)(2,1)S(1)}, u32[]{:S(2)}, u32[]{:S(2)}) collective-permute-start(bf16[1,32,2048]{2,1,0:T(8,128)(2,1)S(1)} %get-tuple-element.1286), channel_id=1, source_target_pairs={{0,16},{1,17},{2,18},{3,19},{4,20},{5,21},{6,22},{7,23},{8,24},{9,... | collective-permute-start | bytes 393224 | tf_op jit(solution)/shard_map/while/body/eval_jaxpr/ppermute | solution.py:14
  204.8 203.3 %while.43 = (s32[]{:T(128)}, bf16[1,32,2048]{2,1,0:T(8,128)(2,1)S(1)}, bf16[1,32,2048]{2,1,0:T(8,128)(2,1)S(1)}, bf16[4,1,32,2048]{3,2,1,0:T(8,128)(2,1)S(1)}, f...) while((s32[]{:T(128)}, ...), condition=%wide.region_19.20_spmd.clone, body=%wide.region_7.19_spmd.clone.sunk | while | flops 417616544 | bytes 54182452 | solution.py:150
  207.6 30.0 %psum.15 = f32[2048]{0:T(1024)S(1)} all-reduce(f32[2048]{0:T(1024)S(1)} %get-tuple-element.1162), channel_id=1, replica_groups=mesh['section'=2,'fsdp'=16] {'fsdp'}, use_global_device_ids=true, to_apply=%region_18.18 | all-reduce | flops 2048 | bytes 16384 | tf_op jit(solution)/shard_map/while/body/eval_jaxpr/psum | solution.py:146
  237.8 9.8 %conditional.6 = (bf16[1,32,2048]{2,1,0:T(8,128)(2,1)S(1)}, bf16[1,32,2048]{2,1,0:T(8,128)(2,1)S(1)}, f32[2048]{0:T(1024)S(1)}) conditional(s32[]{:T(128)} %convert_element_type.399, () %tuple.124, (bf16[4,1,32,2048]{3,2,1,0:T(8,128)(2,1)S(1)}, s32[]{:T(128)}, pred[1,32,2048]{2,1,0:T(32,128)(4,1)S(1)}, bf16[1,32,2048]{2,1,0:T(8,128)(2,1)S(1)}, ...), branch_computations={%region_8.8_spmd, %region_9.17_spmd} | conditional | flops 417282720 | bytes 51716228 | solution.py:140
  239.0 3.1 fusion.38
  250.3 30.0 %psum.15 = f32[2048]{0:T(1024)S(1)} all-reduce(f32[2048]{0:T(1024)S(1)} %get-tuple-element.1162), channel_id=1, replica_groups=mesh['section'=2,'fsdp'=16] {'fsdp'}, use_global_device_ids=true, to_apply=%region_18.18 | all-reduce | flops 2048 | bytes 16384 | tf_op jit(solution)/shard_map/while/body/eval_jaxpr/psum | solution.py:146
  280.4 9.8 %conditional.6 = (bf16[1,32,2048]{2,1,0:T(8,128)(2,1)S(1)}, bf16[1,32,2048]{2,1,0:T(8,128)(2,1)S(1)}, f32[2048]{0:T(1024)S(1)}) conditional(s32[]{:T(128)} %convert_element_type.399, () %tuple.124, (bf16[4,1,32,2048]{3,2,1,0:T(8,128)(2,1)S(1)}, s32[]{:T(128)}, pred[1,32,2048]{2,1,0:T(32,128)(4,1)S(1)}, bf16[1,32,2048]{2,1,0:T(8,128)(2,1)S(1)}, ...), branch_computations={%region_8.8_spmd, %region_9.17_spmd} | conditional | flops 417282720 | bytes 51716228 | solution.py:140
  281.6 3.1 fusion.38
  292.9 30.0 %psum.15 = f32[2048]{0:T(1024)S(1)} all-reduce(f32[2048]{0:T(1024)S(1)} %get-tuple-element.1162), channel_id=1, replica_groups=mesh['section'=2,'fsdp'=16] {'fsdp'}, use_global_device_ids=true, to_apply=%region_18.18 | all-reduce | flops 2048 | bytes 16384 | tf_op jit(solution)/shard_map/while/body/eval_jaxpr/psum | solution.py:146
  323.0 9.8 %conditional.6 = (bf16[1,32,2048]{2,1,0:T(8,128)(2,1)S(1)}, bf16[1,32,2048]{2,1,0:T(8,128)(2,1)S(1)}, f32[2048]{0:T(1024)S(1)}) conditional(s32[]{:T(128)} %convert_element_type.399, () %tuple.124, (bf16[4,1,32,2048]{3,2,1,0:T(8,128)(2,1)S(1)}, s32[]{:T(128)}, pred[1,32,2048]{2,1,0:T(32,128)(4,1)S(1)}, bf16[1,32,2048]{2,1,0:T(8,128)(2,1)S(1)}, ...), branch_computations={%region_8.8_spmd, %region_9.17_spmd} | conditional | flops 417282720 | bytes 51716228 | solution.py:140
  324.2 3.1 fusion.38
  335.5 30.0 %psum.15 = f32[2048]{0:T(1024)S(1)} all-reduce(f32[2048]{0:T(1024)S(1)} %get-tuple-element.1162), channel_id=1, replica_groups=mesh['section'=2,'fsdp'=16] {'fsdp'}, use_global_device_ids=true, to_apply=%region_18.18 | all-reduce | flops 2048 | bytes 16384 | tf_op jit(solution)/shard_map/while/body/eval_jaxpr/psum | solution.py:146
  365.6 9.8 %conditional.6 = (bf16[1,32,2048]{2,1,0:T(8,128)(2,1)S(1)}, bf16[1,32,2048]{2,1,0:T(8,128)(2,1)S(1)}, f32[2048]{0:T(1024)S(1)}) conditional(s32[]{:T(128)} %convert_element_type.399, () %tuple.124, (bf16[4,1,32,2048]{3,2,1,0:T(8,128)(2,1)S(1)}, s32[]{:T(128)}, pred[1,32,2048]{2,1,0:T(32,128)(4,1)S(1)}, bf16[1,32,2048]{2,1,0:T(8,128)(2,1)S(1)}, ...), branch_computations={%region_8.8_spmd, %region_9.17_spmd} | conditional | flops 417282720 | bytes 51716228 | solution.py:140
  366.8 3.1 fusion.38
  378.1 30.0 %psum.15 = f32[2048]{0:T(1024)S(1)} all-reduce(f32[2048]{0:T(1024)S(1)} %get-tuple-element.1162), channel_id=1, replica_groups=mesh['section'=2,'fsdp'=16] {'fsdp'}, use_global_device_ids=true, to_apply=%region_18.18 | all-reduce | flops 2048 | bytes 16384 | tf_op jit(solution)/shard_map/while/body/eval_jaxpr/psum | solution.py:146
  (294 shorter events, 82.0 us)
Async XLA Ops:
  7.2 56.3 %all-gather.3.cloned.1.call-start = ((), (), s32[]{:S(2)}) async-start(), calls=%async_computation | async-start | bytes 4456448 | tf_op jit(solution)/shard_map/all_gather | solution.py:65
  7.9 106.8 %all-gather.5.cloned.1.call-start = ((), (), s32[]{:S(2)}) async-start(), calls=%async_computation.1 | async-start | bytes 4456448 | tf_op jit(solution)/shard_map/all_gather | solution.py:64
  114.9 89.9 %copy-start.4 = (bf16[4,1,32,2048]{3,2,1,0:T(8,128)(2,1)S(1)}, bf16[4,1,32,2048]{3,2,1,0:T(8,128)(2,1)}, u32[]{:S(2)}) copy-start(bf16[4,1,32,2048]{3,2,1,0:T(8,128)(2,1)} %param.23) | copy-start | bytes 1572868
  124.3 7.6 %collective-permute-start = (bf16[1,32,2048]{2,1,0:T(8,128)(2,1)S(1)}, bf16[1,32,2048]{2,1,0:T(8,128)(2,1)S(1)}, u32[]{:S(2)}, u32[]{:S(2)}) collective-permute-start(bf16[1,32,2048]{2,1,0:T(8,128)(2,1)S(1)} %get-tuple-element.1286), channel_id=1, source_target_pairs={{0,16},{1,17},{2,18},{3,19},{4,20},{5,21},{6,22},{7,23},{8,24},{9,... | collective-permute-start | bytes 393224 | tf_op jit(solution)/shard_map/while/body/eval_jaxpr/ppermute | solution.py:14
  125.6 6.2 %collective-permute-start.1 = (bf16[1,32,2048]{2,1,0:T(8,128)(2,1)S(1)}, bf16[1,32,2048]{2,1,0:T(8,128)(2,1)S(1)}, u32[]{:S(2)}, u32[]{:S(2)}) collective-permute-start(bf16[1,32,2048]{2,1,0:T(8,128)(2,1)S(1)} %select_select_fusion.2), channel_id=1, source_target_pairs={{0,16},{1,17},{2,18},{3,19},{4,20},{5,21},{6,22},{7,23},{8,24},{9,... | collective-permute-start | bytes 393224 | tf_op jit(solution)/shard_map/while/body/eval_jaxpr/ppermute | solution.py:14
  141.2 9.9 %collective-permute-start = (bf16[1,32,2048]{2,1,0:T(8,128)(2,1)S(1)}, bf16[1,32,2048]{2,1,0:T(8,128)(2,1)S(1)}, u32[]{:S(2)}, u32[]{:S(2)}) collective-permute-start(bf16[1,32,2048]{2,1,0:T(8,128)(2,1)S(1)} %get-tuple-element.1286), channel_id=1, source_target_pairs={{0,16},{1,17},{2,18},{3,19},{4,20},{5,21},{6,22},{7,23},{8,24},{9,... | collective-permute-start | bytes 393224 | tf_op jit(solution)/shard_map/while/body/eval_jaxpr/ppermute | solution.py:14
  145.6 5.4 %collective-permute-start.1 = (bf16[1,32,2048]{2,1,0:T(8,128)(2,1)S(1)}, bf16[1,32,2048]{2,1,0:T(8,128)(2,1)S(1)}, u32[]{:S(2)}, u32[]{:S(2)}) collective-permute-start(bf16[1,32,2048]{2,1,0:T(8,128)(2,1)S(1)} %select_select_fusion.2), channel_id=1, source_target_pairs={{0,16},{1,17},{2,18},{3,19},{4,20},{5,21},{6,22},{7,23},{8,24},{9,... | collective-permute-start | bytes 393224 | tf_op jit(solution)/shard_map/while/body/eval_jaxpr/ppermute | solution.py:14
  160.4 9.0 %collective-permute-start = (bf16[1,32,2048]{2,1,0:T(8,128)(2,1)S(1)}, bf16[1,32,2048]{2,1,0:T(8,128)(2,1)S(1)}, u32[]{:S(2)}, u32[]{:S(2)}) collective-permute-start(bf16[1,32,2048]{2,1,0:T(8,128)(2,1)S(1)} %get-tuple-element.1286), channel_id=1, source_target_pairs={{0,16},{1,17},{2,18},{3,19},{4,20},{5,21},{6,22},{7,23},{8,24},{9,... | collective-permute-start | bytes 393224 | tf_op jit(solution)/shard_map/while/body/eval_jaxpr/ppermute | solution.py:14
  164.8 4.5 %collective-permute-start.1 = (bf16[1,32,2048]{2,1,0:T(8,128)(2,1)S(1)}, bf16[1,32,2048]{2,1,0:T(8,128)(2,1)S(1)}, u32[]{:S(2)}, u32[]{:S(2)}) collective-permute-start(bf16[1,32,2048]{2,1,0:T(8,128)(2,1)S(1)} %select_select_fusion.2), channel_id=1, source_target_pairs={{0,16},{1,17},{2,18},{3,19},{4,20},{5,21},{6,22},{7,23},{8,24},{9,... | collective-permute-start | bytes 393224 | tf_op jit(solution)/shard_map/while/body/eval_jaxpr/ppermute | solution.py:14
  178.8 8.3 %collective-permute-start = (bf16[1,32,2048]{2,1,0:T(8,128)(2,1)S(1)}, bf16[1,32,2048]{2,1,0:T(8,128)(2,1)S(1)}, u32[]{:S(2)}, u32[]{:S(2)}) collective-permute-start(bf16[1,32,2048]{2,1,0:T(8,128)(2,1)S(1)} %get-tuple-element.1286), channel_id=1, source_target_pairs={{0,16},{1,17},{2,18},{3,19},{4,20},{5,21},{6,22},{7,23},{8,24},{9,... | collective-permute-start | bytes 393224 | tf_op jit(solution)/shard_map/while/body/eval_jaxpr/ppermute | solution.py:14
  183.2 3.8 collective-permute-start.1
  188.2 16.5 %collective-permute-start = (bf16[1,32,2048]{2,1,0:T(8,128)(2,1)S(1)}, bf16[1,32,2048]{2,1,0:T(8,128)(2,1)S(1)}, u32[]{:S(2)}, u32[]{:S(2)}) collective-permute-start(bf16[1,32,2048]{2,1,0:T(8,128)(2,1)S(1)} %get-tuple-element.1286), channel_id=1, source_target_pairs={{0,16},{1,17},{2,18},{3,19},{4,20},{5,21},{6,22},{7,23},{8,24},{9,... | collective-permute-start | bytes 393224 | tf_op jit(solution)/shard_map/while/body/eval_jaxpr/ppermute | solution.py:14
  200.8 3.8 collective-permute-start.1
  205.0 32.7 %collective-permute-start.2 = (bf16[1,32,2048]{2,1,0:T(8,128)(2,1)S(1)}, bf16[1,32,2048]{2,1,0:T(8,128)(2,1)S(1)}, u32[]{:S(2)}, u32[]{:S(2)}) collective-permute-start(bf16[1,32,2048]{2,1,0:T(8,128)(2,1)S(1)} %get-tuple-element.1160), channel_id=1, source_target_pairs={{16,0},{17,1},{18,2},{19,3},{20,4},{21,5},{22,6},{23,7},{24,8},{25... | collective-permute-start | bytes 393224 | tf_op jit(solution)/shard_map/while/body/eval_jaxpr/ppermute | solution.py:14
  206.3 31.4 %collective-permute-start.3 = (bf16[1,32,2048]{2,1,0:T(8,128)(2,1)S(1)}, bf16[1,32,2048]{2,1,0:T(8,128)(2,1)S(1)}, u32[]{:S(2)}, u32[]{:S(2)}) collective-permute-start(bf16[1,32,2048]{2,1,0:T(8,128)(2,1)S(1)} %get-tuple-element.1161), channel_id=1, source_target_pairs={{16,0},{17,1},{18,2},{19,3},{20,4},{21,5},{22,6},{23,7},{24,8},{25... | collective-permute-start | bytes 393224 | tf_op jit(solution)/shard_map/while/body/eval_jaxpr/ppermute | solution.py:14
  237.8 5.4 %copy-start.2 = (bf16[1024,2048]{1,0:T(8,128)(2,1)S(1)}, bf16[1024,2048]{1,0:T(8,128)(2,1)}, u32[]{:S(2)}) copy-start(bf16[1024,2048]{1,0:T(8,128)(2,1)} %get-tuple-element.750) | copy-start | bytes 12582916 | tf_op jit(solution)/shard_map/while/body/eval_jaxpr/cond
  242.1 3.1 copy-start.3
  242.1 3.6 copy-start.1
  247.6 32.7 %collective-permute-start.2 = (bf16[1,32,2048]{2,1,0:T(8,128)(2,1)S(1)}, bf16[1,32,2048]{2,1,0:T(8,128)(2,1)S(1)}, u32[]{:S(2)}, u32[]{:S(2)}) collective-permute-start(bf16[1,32,2048]{2,1,0:T(8,128)(2,1)S(1)} %get-tuple-element.1160), channel_id=1, source_target_pairs={{16,0},{17,1},{18,2},{19,3},{20,4},{21,5},{22,6},{23,7},{24,8},{25... | collective-permute-start | bytes 393224 | tf_op jit(solution)/shard_map/while/body/eval_jaxpr/ppermute | solution.py:14
  248.9 31.4 %collective-permute-start.3 = (bf16[1,32,2048]{2,1,0:T(8,128)(2,1)S(1)}, bf16[1,32,2048]{2,1,0:T(8,128)(2,1)S(1)}, u32[]{:S(2)}, u32[]{:S(2)}) collective-permute-start(bf16[1,32,2048]{2,1,0:T(8,128)(2,1)S(1)} %get-tuple-element.1161), channel_id=1, source_target_pairs={{16,0},{17,1},{18,2},{19,3},{20,4},{21,5},{22,6},{23,7},{24,8},{25... | collective-permute-start | bytes 393224 | tf_op jit(solution)/shard_map/while/body/eval_jaxpr/ppermute | solution.py:14
  280.4 5.4 %copy-start.2 = (bf16[1024,2048]{1,0:T(8,128)(2,1)S(1)}, bf16[1024,2048]{1,0:T(8,128)(2,1)}, u32[]{:S(2)}) copy-start(bf16[1024,2048]{1,0:T(8,128)(2,1)} %get-tuple-element.750) | copy-start | bytes 12582916 | tf_op jit(solution)/shard_map/while/body/eval_jaxpr/cond
  284.8 3.6 copy-start.1
  290.2 32.7 %collective-permute-start.2 = (bf16[1,32,2048]{2,1,0:T(8,128)(2,1)S(1)}, bf16[1,32,2048]{2,1,0:T(8,128)(2,1)S(1)}, u32[]{:S(2)}, u32[]{:S(2)}) collective-permute-start(bf16[1,32,2048]{2,1,0:T(8,128)(2,1)S(1)} %get-tuple-element.1160), channel_id=1, source_target_pairs={{16,0},{17,1},{18,2},{19,3},{20,4},{21,5},{22,6},{23,7},{24,8},{25... | collective-permute-start | bytes 393224 | tf_op jit(solution)/shard_map/while/body/eval_jaxpr/ppermute | solution.py:14
  291.5 31.4 %collective-permute-start.3 = (bf16[1,32,2048]{2,1,0:T(8,128)(2,1)S(1)}, bf16[1,32,2048]{2,1,0:T(8,128)(2,1)S(1)}, u32[]{:S(2)}, u32[]{:S(2)}) collective-permute-start(bf16[1,32,2048]{2,1,0:T(8,128)(2,1)S(1)} %get-tuple-element.1161), channel_id=1, source_target_pairs={{16,0},{17,1},{18,2},{19,3},{20,4},{21,5},{22,6},{23,7},{24,8},{25... | collective-permute-start | bytes 393224 | tf_op jit(solution)/shard_map/while/body/eval_jaxpr/ppermute | solution.py:14
  323.0 5.4 %copy-start.2 = (bf16[1024,2048]{1,0:T(8,128)(2,1)S(1)}, bf16[1024,2048]{1,0:T(8,128)(2,1)}, u32[]{:S(2)}) copy-start(bf16[1024,2048]{1,0:T(8,128)(2,1)} %get-tuple-element.750) | copy-start | bytes 12582916 | tf_op jit(solution)/shard_map/while/body/eval_jaxpr/cond
  327.4 3.6 copy-start.1
  332.8 32.7 %collective-permute-start.2 = (bf16[1,32,2048]{2,1,0:T(8,128)(2,1)S(1)}, bf16[1,32,2048]{2,1,0:T(8,128)(2,1)S(1)}, u32[]{:S(2)}, u32[]{:S(2)}) collective-permute-start(bf16[1,32,2048]{2,1,0:T(8,128)(2,1)S(1)} %get-tuple-element.1160), channel_id=1, source_target_pairs={{16,0},{17,1},{18,2},{19,3},{20,4},{21,5},{22,6},{23,7},{24,8},{25... | collective-permute-start | bytes 393224 | tf_op jit(solution)/shard_map/while/body/eval_jaxpr/ppermute | solution.py:14
  334.1 31.4 %collective-permute-start.3 = (bf16[1,32,2048]{2,1,0:T(8,128)(2,1)S(1)}, bf16[1,32,2048]{2,1,0:T(8,128)(2,1)S(1)}, u32[]{:S(2)}, u32[]{:S(2)}) collective-permute-start(bf16[1,32,2048]{2,1,0:T(8,128)(2,1)S(1)} %get-tuple-element.1161), channel_id=1, source_target_pairs={{16,0},{17,1},{18,2},{19,3},{20,4},{21,5},{22,6},{23,7},{24,8},{25... | collective-permute-start | bytes 393224 | tf_op jit(solution)/shard_map/while/body/eval_jaxpr/ppermute | solution.py:14
  365.6 5.4 %copy-start.2 = (bf16[1024,2048]{1,0:T(8,128)(2,1)S(1)}, bf16[1024,2048]{1,0:T(8,128)(2,1)}, u32[]{:S(2)}) copy-start(bf16[1024,2048]{1,0:T(8,128)(2,1)} %get-tuple-element.750) | copy-start | bytes 12582916 | tf_op jit(solution)/shard_map/while/body/eval_jaxpr/cond
  370.0 3.6 copy-start.1
  375.4 32.7 %collective-permute-start.2 = (bf16[1,32,2048]{2,1,0:T(8,128)(2,1)S(1)}, bf16[1,32,2048]{2,1,0:T(8,128)(2,1)S(1)}, u32[]{:S(2)}, u32[]{:S(2)}) collective-permute-start(bf16[1,32,2048]{2,1,0:T(8,128)(2,1)S(1)} %get-tuple-element.1160), channel_id=1, source_target_pairs={{16,0},{17,1},{18,2},{19,3},{20,4},{21,5},{22,6},{23,7},{24,8},{25... | collective-permute-start | bytes 393224 | tf_op jit(solution)/shard_map/while/body/eval_jaxpr/ppermute | solution.py:14
  376.7 31.4 %collective-permute-start.3 = (bf16[1,32,2048]{2,1,0:T(8,128)(2,1)S(1)}, bf16[1,32,2048]{2,1,0:T(8,128)(2,1)S(1)}, u32[]{:S(2)}, u32[]{:S(2)}) collective-permute-start(bf16[1,32,2048]{2,1,0:T(8,128)(2,1)S(1)} %get-tuple-element.1161), channel_id=1, source_target_pairs={{16,0},{17,1},{18,2},{19,3},{20,4},{21,5},{22,6},{23,7},{24,8},{25... | collective-permute-start | bytes 393224 | tf_op jit(solution)/shard_map/while/body/eval_jaxpr/ppermute | solution.py:14
  (6 other events, 13.3 us)
Sparse Core Ops, SparseCore 0:
  10.2 53.2 all-gather.2
  65.6 49.0 all-gather.4
where the time goes:
time: 417 us; the launch traced here: 416 us
  blocking collectives  150 us (36%)
  waiting for transfers between devices  123 us (29%)
  matrix products  54.3 us (13%)
  starting transfers between devices  46.6 us (11%)
  other arithmetic  22.1 us (5%)
  between operations  14.2 us (3%)
    psum x5, blocking collectives, backward_tick(): gain_total = gain_total + lax.psum(gain_grad, 'fsdp')  150 us
    all_gather x1, waiting for transfers between devices, on_device(): lax.all_gather(output_weights, 'fsdp', axis=1, tiled=True)  53.6 us
    all_gather x1, waiting for transfers between devices, on_device(): lax.all_gather(query_weights, 'fsdp', axis=1, tiled=True)  51.2 us
    ppermute x20, starting transfers between devices, shifted(): return lax.ppermute(array, axis, pairs)  46.5 us
    dot_general x12, matrix products, attend_layer(): jnp.dot(normed_rows, query_weight, preferred_element_type=jnp.float32)  30.8 us
    dot_general x8, matrix products, attend_layer(): update = jnp.dot(mixed, output_weight, preferred_element_type=jnp.float32)  17.4 us
    ppermute x20, waiting for transfers between devices, shifted(): return lax.ppermute(array, axis, pairs)  17 us
  transfers between devices with their start and end apart: 22, of which 7 were waited for; matrix products, arithmetic and copies ran while one was open for 0% of the time, Pallas kernels for 0%

commit v1 on v0

--- a/solution.py
+++ b/solution.py
@@ -143,7 +143,7 @@
         send_side = jnp.where(is_decoder & (section_index != half_sections), memory_sum, zero_act)
         got_grad, got_memory_grad = shifted((send_main, send_side), "section", -1)
         grads_buf = place_slot(grads_buf, slot, input_grad, is_active)
-        gain_total = gain_total + lax.psum(gain_grad, "fsdp")
+        gain_total = gain_total + jnp.sum(lax.all_gather(gain_grad, "fsdp"), axis=0)
         return (got_grad, got_memory_grad, grads_buf, gain_total)
 
     back_state = (zero_act, zero_act, zero_stack, jnp.zeros_like(gain_vector))

time: 417 us -> 361 us (0.87)
  blocking collectives: 150 us -> 93.1 us
    psum x5 -> x0, blocking collectives: 150 us -> none  [backward_tick(): gain_total = gain_total + lax.psum(gain_grad, 'fsdp')]
    all_gather x0 -> x5, blocking collectives: none -> 93.1 us  [backward_tick(): gain_total = gain_total + jnp.sum(lax.all_gather(gain_grad, 'fsdp'), axis=0)]
  transfers between devices with their start and end apart: 22 -> 22, of which waited for: 7 -> 7; matrix products, arithmetic and copies ran while one was open for 0% -> 1% of each run, Pallas kernels for 0% -> 0%
where the time goes in v1:
time: 361 us; the launch traced here: 359 us
  waiting for transfers between devices  123 us (34%)
  blocking collectives  93.1 us (26%)
  matrix products  54.3 us (15%)
  starting transfers between devices  46.6 us (13%)
  other arithmetic  22.2 us (6%)
  between operations  14.2 us (4%)
    all_gather x5, blocking collectives, backward_tick(): gain_total = gain_total + jnp.sum(lax.all_gather(gain_grad, 'fsdp'), axis=0)  93.1 us
    all_gather x1, waiting for transfers between devices, on_device(): lax.all_gather(output_weights, 'fsdp', axis=1, tiled=True)  53.6 us
    all_gather x1, waiting for transfers between devices, on_device(): lax.all_gather(query_weights, 'fsdp', axis=1, tiled=True)  51.2 us
    ppermute x20, starting transfers between devices, shifted(): return lax.ppermute(array, axis, pairs)  46.5 us
    dot_general x12, matrix products, attend_layer(): jnp.dot(normed_rows, query_weight, preferred_element_type=jnp.float32)  30.8 us
    dot_general x8, matrix products, attend_layer(): update = jnp.dot(mixed, output_weight, preferred_element_type=jnp.float32)  17.4 us
    ppermute x20, waiting for transfers between devices, shifted(): return lax.ppermute(array, axis, pairs)  17 us
  transfers between devices with their start and end apart: 22, of which 7 were waited for; matrix products, arithmetic and copies ran while one was open for 1% of the time, Pallas kernels for 0%

profile of v1, /device:TPU:0, one launch (start us, length us, event | category | flops | bytes accessed | tf_op | source)
XLA Modules:
  0.0 359.2 jit_solution(16348101874996884516)
XLA Ops:
  9.9 53.6 %all-gather.7.cloned.1.call-done = bf16[1,1024,2048]{2,1,0:T(8,128)(2,1)} async-done(((bf16[1,64,2048]{2,1,0:T(8,128)(2,1)}), bf16[1,1024,2048]{2,1,0:T(8,128)(2,1)}) %all-gather.7.cloned.1.call-update) | async-done | bytes 4194320 | tf_op jit(solution)/shard_map/all_gather | solution.py:65
  63.5 51.2 %all-gather.9.cloned.1.call-done = bf16[1,2048,1024]{2,1,0:T(8,128)(2,1)} async-done(((bf16[1,128,1024]{2,1,0:T(8,128)(2,1)}), bf16[1,2048,1024]{2,1,0:T(8,128)(2,1)}) %all-gather.9.cloned.1.call-update) | async-done | bytes 4194320 | tf_op jit(solution)/shard_map/all_gather | solution.py:64
  114.9 89.8 %while.42 = (s32[]{:T(128)}, bf16[1,32,2048]{2,1,0:T(8,128)(2,1)S(1)}, bf16[1,32,2048]{2,1,0:T(8,128)(2,1)S(1)}, bf16[4,1,32,2048]{3,2,1,0:T(8,128)(2,1)S(1)}, b...) while((s32[]{:T(128)}, ...), condition=%wide.region_6.7_spmd, body=%wide.region_0.6_spmd.sunk | while | flops 274366848 | bytes 14173985 | solution.py:113
  116.0 8.3 %conditional.5 = (bf16[1,32,2048]{2,1,0:T(8,128)(2,1)S(1)}) conditional(s32[]{:T(128)} %convert_element_type.398, () %tuple.122, (bf16[1,32,2048]{2,1,0:T(8,128)(2,1)S(1)}, pred[1,32,2048]{2,1,0:T(8,128)(4,1)S(1)}, bf16[1,32,2048]{2,1,0:T(8,128)(2,1)S(1)}, f32[1,2048]{1,0:T(1,128)}, bf16[2048,1024]{1,0:T(8,128)(2,1)}, ...), branch_computations={%region_1.1_spmd, %region_2.5_spmd} | conditional | flops 273973632 | bytes 10700172 | solution.py:103
  117.0 3.1 fusion.5
  127.0 4.8 %collective-permute-done.1 = bf16[1,32,2048]{2,1,0:T(8,128)(2,1)S(1)} collective-permute-done((bf16[1,32,2048]{2,1,0:T(8,128)(2,1)S(1)}, bf16[1,32,2048]{2,1,0:T(8,128)(2,1)S(1)}, u32[]{:S(2)}, u32[]{:S(2)}) %collective-permute-start.1) | collective-permute-done | bytes 131104 | tf_op jit(solution)/shard_map/while/body/eval_jaxpr/ppermute | solution.py:14
  132.9 8.3 %conditional.5 = (bf16[1,32,2048]{2,1,0:T(8,128)(2,1)S(1)}) conditional(s32[]{:T(128)} %convert_element_type.398, () %tuple.122, (bf16[1,32,2048]{2,1,0:T(8,128)(2,1)S(1)}, pred[1,32,2048]{2,1,0:T(8,128)(4,1)S(1)}, bf16[1,32,2048]{2,1,0:T(8,128)(2,1)S(1)}, f32[1,2048]{1,0:T(1,128)}, bf16[2048,1024]{1,0:T(8,128)(2,1)}, ...), branch_computations={%region_1.1_spmd, %region_2.5_spmd} | conditional | flops 273973632 | bytes 10700172 | solution.py:103
  134.0 3.1 fusion.5
  141.2 4.4 %collective-permute-start = (bf16[1,32,2048]{2,1,0:T(8,128)(2,1)S(1)}, bf16[1,32,2048]{2,1,0:T(8,128)(2,1)S(1)}, u32[]{:S(2)}, u32[]{:S(2)}) collective-permute-start(bf16[1,32,2048]{2,1,0:T(8,128)(2,1)S(1)} %get-tuple-element.1319), channel_id=1, source_target_pairs={{0,16},{1,17},{2,18},{3,19},{4,20},{5,21},{6,22},{7,23},{8,24},{9,... | collective-permute-start | bytes 393224 | tf_op jit(solution)/shard_map/while/body/eval_jaxpr/ppermute | solution.py:14
  147.0 4.0 %collective-permute-done.1 = bf16[1,32,2048]{2,1,0:T(8,128)(2,1)S(1)} collective-permute-done((bf16[1,32,2048]{2,1,0:T(8,128)(2,1)S(1)}, bf16[1,32,2048]{2,1,0:T(8,128)(2,1)S(1)}, u32[]{:S(2)}, u32[]{:S(2)}) %collective-permute-start.1) | collective-permute-done | bytes 131104 | tf_op jit(solution)/shard_map/while/body/eval_jaxpr/ppermute | solution.py:14
  152.1 8.3 %conditional.5 = (bf16[1,32,2048]{2,1,0:T(8,128)(2,1)S(1)}) conditional(s32[]{:T(128)} %convert_element_type.398, () %tuple.122, (bf16[1,32,2048]{2,1,0:T(8,128)(2,1)S(1)}, pred[1,32,2048]{2,1,0:T(8,128)(4,1)S(1)}, bf16[1,32,2048]{2,1,0:T(8,128)(2,1)S(1)}, f32[1,2048]{1,0:T(1,128)}, bf16[2048,1024]{1,0:T(8,128)(2,1)}, ...), branch_computations={%region_1.1_spmd, %region_2.5_spmd} | conditional | flops 273973632 | bytes 10700172 | solution.py:103
  153.2 3.1 fusion.5
  160.4 4.4 %collective-permute-start = (bf16[1,32,2048]{2,1,0:T(8,128)(2,1)S(1)}, bf16[1,32,2048]{2,1,0:T(8,128)(2,1)S(1)}, u32[]{:S(2)}, u32[]{:S(2)}) collective-permute-start(bf16[1,32,2048]{2,1,0:T(8,128)(2,1)S(1)} %get-tuple-element.1319), channel_id=1, source_target_pairs={{0,16},{1,17},{2,18},{3,19},{4,20},{5,21},{6,22},{7,23},{8,24},{9,... | collective-permute-start | bytes 393224 | tf_op jit(solution)/shard_map/while/body/eval_jaxpr/ppermute | solution.py:14
  166.2 3.2 collective-permute-done.1
  170.5 8.3 %conditional.5 = (bf16[1,32,2048]{2,1,0:T(8,128)(2,1)S(1)}) conditional(s32[]{:T(128)} %convert_element_type.398, () %tuple.122, (bf16[1,32,2048]{2,1,0:T(8,128)(2,1)S(1)}, pred[1,32,2048]{2,1,0:T(8,128)(4,1)S(1)}, bf16[1,32,2048]{2,1,0:T(8,128)(2,1)S(1)}, f32[1,2048]{1,0:T(1,128)}, bf16[2048,1024]{1,0:T(8,128)(2,1)}, ...), branch_computations={%region_1.1_spmd, %region_2.5_spmd} | conditional | flops 273973632 | bytes 10700172 | solution.py:103
  171.5 3.1 fusion.5
  178.8 4.4 %collective-permute-start = (bf16[1,32,2048]{2,1,0:T(8,128)(2,1)S(1)}, bf16[1,32,2048]{2,1,0:T(8,128)(2,1)S(1)}, u32[]{:S(2)}, u32[]{:S(2)}) collective-permute-start(bf16[1,32,2048]{2,1,0:T(8,128)(2,1)S(1)} %get-tuple-element.1319), channel_id=1, source_target_pairs={{0,16},{1,17},{2,18},{3,19},{4,20},{5,21},{6,22},{7,23},{8,24},{9,... | collective-permute-start | bytes 393224 | tf_op jit(solution)/shard_map/while/body/eval_jaxpr/ppermute | solution.py:14
  188.2 12.6 %collective-permute-start = (bf16[1,32,2048]{2,1,0:T(8,128)(2,1)S(1)}, bf16[1,32,2048]{2,1,0:T(8,128)(2,1)S(1)}, u32[]{:S(2)}, u32[]{:S(2)}) collective-permute-start(bf16[1,32,2048]{2,1,0:T(8,128)(2,1)S(1)} %get-tuple-element.1319), channel_id=1, source_target_pairs={{0,16},{1,17},{2,18},{3,19},{4,20},{5,21},{6,22},{7,23},{8,24},{9,... | collective-permute-start | bytes 393224 | tf_op jit(solution)/shard_map/while/body/eval_jaxpr/ppermute | solution.py:14
  204.8 146.7 %while.43 = (s32[]{:T(128)}, bf16[1,32,2048]{2,1,0:T(8,128)(2,1)S(1)}, bf16[1,32,2048]{2,1,0:T(8,128)(2,1)S(1)}, bf16[4,1,32,2048]{3,2,1,0:T(8,128)(2,1)S(1)}, f...) while((s32[]{:T(128)}, ...), condition=%wide.region_19.20_spmd.clone, body=%wide.region_7.19_spmd.clone.sunk | while | flops 417645216 | bytes 54706752 | solution.py:150
  207.6 19.3 %all-gather.3 = f32[32768]{0:T(1024)S(1)} all-gather(f32[2048]{0:T(1024)S(1)} %get-tuple-element.1192), channel_id=2, replica_groups=mesh['section'=2,'fsdp'=16] {'fsdp'}, dimensions={0}, use_global_device_ids=true | all-gather | bytes 139264 | tf_op jit(solution)/shard_map/while/body/eval_jaxpr/all_gather | solution.py:146
  227.1 9.8 %conditional.6 = (bf16[1,32,2048]{2,1,0:T(8,128)(2,1)S(1)}, bf16[1,32,2048]{2,1,0:T(8,128)(2,1)S(1)}, f32[2048]{0:T(1024)S(1)}) conditional(s32[]{:T(128)} %convert_element_type.399, () %tuple.126, (bf16[4,1,32,2048]{3,2,1,0:T(8,128)(2,1)S(1)}, s32[]{:T(128)}, pred[1,32,2048]{2,1,0:T(32,128)(4,1)S(1)}, bf16[1,32,2048]{2,1,0:T(8,128)(2,1)S(1)}, ...), branch_computations={%region_8.8_spmd, %region_9.17_spmd} | conditional | flops 417282720 | bytes 51716228 | solution.py:140
  228.3 3.1 fusion.38
  239.6 17.8 %all-gather.3 = f32[32768]{0:T(1024)S(1)} all-gather(f32[2048]{0:T(1024)S(1)} %get-tuple-element.1192), channel_id=2, replica_groups=mesh['section'=2,'fsdp'=16] {'fsdp'}, dimensions={0}, use_global_device_ids=true | all-gather | bytes 139264 | tf_op jit(solution)/shard_map/while/body/eval_jaxpr/all_gather | solution.py:146
  257.6 9.8 %conditional.6 = (bf16[1,32,2048]{2,1,0:T(8,128)(2,1)S(1)}, bf16[1,32,2048]{2,1,0:T(8,128)(2,1)S(1)}, f32[2048]{0:T(1024)S(1)}) conditional(s32[]{:T(128)} %convert_element_type.399, () %tuple.126, (bf16[4,1,32,2048]{3,2,1,0:T(8,128)(2,1)S(1)}, s32[]{:T(128)}, pred[1,32,2048]{2,1,0:T(32,128)(4,1)S(1)}, bf16[1,32,2048]{2,1,0:T(8,128)(2,1)S(1)}, ...), branch_computations={%region_8.8_spmd, %region_9.17_spmd} | conditional | flops 417282720 | bytes 51716228 | solution.py:140
  258.8 3.1 fusion.38
  270.1 19.1 %all-gather.3 = f32[32768]{0:T(1024)S(1)} all-gather(f32[2048]{0:T(1024)S(1)} %get-tuple-element.1192), channel_id=2, replica_groups=mesh['section'=2,'fsdp'=16] {'fsdp'}, dimensions={0}, use_global_device_ids=true | all-gather | bytes 139264 | tf_op jit(solution)/shard_map/while/body/eval_jaxpr/all_gather | solution.py:146
  289.4 9.8 %conditional.6 = (bf16[1,32,2048]{2,1,0:T(8,128)(2,1)S(1)}, bf16[1,32,2048]{2,1,0:T(8,128)(2,1)S(1)}, f32[2048]{0:T(1024)S(1)}) conditional(s32[]{:T(128)} %convert_element_type.399, () %tuple.126, (bf16[4,1,32,2048]{3,2,1,0:T(8,128)(2,1)S(1)}, s32[]{:T(128)}, pred[1,32,2048]{2,1,0:T(32,128)(4,1)S(1)}, bf16[1,32,2048]{2,1,0:T(8,128)(2,1)S(1)}, ...), branch_computations={%region_8.8_spmd, %region_9.17_spmd} | conditional | flops 417282720 | bytes 51716228 | solution.py:140
  290.6 3.1 fusion.38
  301.9 17.8 %all-gather.3 = f32[32768]{0:T(1024)S(1)} all-gather(f32[2048]{0:T(1024)S(1)} %get-tuple-element.1192), channel_id=2, replica_groups=mesh['section'=2,'fsdp'=16] {'fsdp'}, dimensions={0}, use_global_device_ids=true | all-gather | bytes 139264 | tf_op jit(solution)/shard_map/while/body/eval_jaxpr/all_gather | solution.py:146
  319.8 9.8 %conditional.6 = (bf16[1,32,2048]{2,1,0:T(8,128)(2,1)S(1)}, bf16[1,32,2048]{2,1,0:T(8,128)(2,1)S(1)}, f32[2048]{0:T(1024)S(1)}) conditional(s32[]{:T(128)} %convert_element_type.399, () %tuple.126, (bf16[4,1,32,2048]{3,2,1,0:T(8,128)(2,1)S(1)}, s32[]{:T(128)}, pred[1,32,2048]{2,1,0:T(32,128)(4,1)S(1)}, bf16[1,32,2048]{2,1,0:T(8,128)(2,1)S(1)}, ...), branch_computations={%region_8.8_spmd, %region_9.17_spmd} | conditional | flops 417282720 | bytes 51716228 | solution.py:140
  321.0 3.1 fusion.38
  332.3 19.1 %all-gather.3 = f32[32768]{0:T(1024)S(1)} all-gather(f32[2048]{0:T(1024)S(1)} %get-tuple-element.1192), channel_id=2, replica_groups=mesh['section'=2,'fsdp'=16] {'fsdp'}, dimensions={0}, use_global_device_ids=true | all-gather | bytes 139264 | tf_op jit(solution)/shard_map/while/body/eval_jaxpr/all_gather | solution.py:146
  (304 shorter events, 82.2 us)
Async XLA Ops:
  7.2 56.3 %all-gather.7.cloned.1.call-start = ((), (), s32[]{:S(2)}) async-start(), calls=%async_computation | async-start | bytes 4456448 | tf_op jit(solution)/shard_map/all_gather | solution.py:65
  7.9 106.8 %all-gather.9.cloned.1.call-start = ((), (), s32[]{:S(2)}) async-start(), calls=%async_computation.1 | async-start | bytes 4456448 | tf_op jit(solution)/shard_map/all_gather | solution.py:64
  114.9 89.9 %copy-start.4 = (bf16[4,1,32,2048]{3,2,1,0:T(8,128)(2,1)S(1)}, bf16[4,1,32,2048]{3,2,1,0:T(8,128)(2,1)}, u32[]{:S(2)}) copy-start(bf16[4,1,32,2048]{3,2,1,0:T(8,128)(2,1)} %param.23) | copy-start | bytes 1572868
  124.3 7.6 %collective-permute-start = (bf16[1,32,2048]{2,1,0:T(8,128)(2,1)S(1)}, bf16[1,32,2048]{2,1,0:T(8,128)(2,1)S(1)}, u32[]{:S(2)}, u32[]{:S(2)}) collective-permute-start(bf16[1,32,2048]{2,1,0:T(8,128)(2,1)S(1)} %get-tuple-element.1319), channel_id=1, source_target_pairs={{0,16},{1,17},{2,18},{3,19},{4,20},{5,21},{6,22},{7,23},{8,24},{9,... | collective-permute-start | bytes 393224 | tf_op jit(solution)/shard_map/while/body/eval_jaxpr/ppermute | solution.py:14
  125.6 6.2 %collective-permute-start.1 = (bf16[1,32,2048]{2,1,0:T(8,128)(2,1)S(1)}, bf16[1,32,2048]{2,1,0:T(8,128)(2,1)S(1)}, u32[]{:S(2)}, u32[]{:S(2)}) collective-permute-start(bf16[1,32,2048]{2,1,0:T(8,128)(2,1)S(1)} %select_select_fusion.2), channel_id=1, source_target_pairs={{0,16},{1,17},{2,18},{3,19},{4,20},{5,21},{6,22},{7,23},{8,24},{9,... | collective-permute-start | bytes 393224 | tf_op jit(solution)/shard_map/while/body/eval_jaxpr/ppermute | solution.py:14
  141.2 9.9 %collective-permute-start = (bf16[1,32,2048]{2,1,0:T(8,128)(2,1)S(1)}, bf16[1,32,2048]{2,1,0:T(8,128)(2,1)S(1)}, u32[]{:S(2)}, u32[]{:S(2)}) collective-permute-start(bf16[1,32,2048]{2,1,0:T(8,128)(2,1)S(1)} %get-tuple-element.1319), channel_id=1, source_target_pairs={{0,16},{1,17},{2,18},{3,19},{4,20},{5,21},{6,22},{7,23},{8,24},{9,... | collective-permute-start | bytes 393224 | tf_op jit(solution)/shard_map/while/body/eval_jaxpr/ppermute | solution.py:14
  145.6 5.4 %collective-permute-start.1 = (bf16[1,32,2048]{2,1,0:T(8,128)(2,1)S(1)}, bf16[1,32,2048]{2,1,0:T(8,128)(2,1)S(1)}, u32[]{:S(2)}, u32[]{:S(2)}) collective-permute-start(bf16[1,32,2048]{2,1,0:T(8,128)(2,1)S(1)} %select_select_fusion.2), channel_id=1, source_target_pairs={{0,16},{1,17},{2,18},{3,19},{4,20},{5,21},{6,22},{7,23},{8,24},{9,... | collective-permute-start | bytes 393224 | tf_op jit(solution)/shard_map/while/body/eval_jaxpr/ppermute | solution.py:14
  160.4 9.0 %collective-permute-start = (bf16[1,32,2048]{2,1,0:T(8,128)(2,1)S(1)}, bf16[1,32,2048]{2,1,0:T(8,128)(2,1)S(1)}, u32[]{:S(2)}, u32[]{:S(2)}) collective-permute-start(bf16[1,32,2048]{2,1,0:T(8,128)(2,1)S(1)} %get-tuple-element.1319), channel_id=1, source_target_pairs={{0,16},{1,17},{2,18},{3,19},{4,20},{5,21},{6,22},{7,23},{8,24},{9,... | collective-permute-start | bytes 393224 | tf_op jit(solution)/shard_map/while/body/eval_jaxpr/ppermute | solution.py:14
  164.8 4.5 %collective-permute-start.1 = (bf16[1,32,2048]{2,1,0:T(8,128)(2,1)S(1)}, bf16[1,32,2048]{2,1,0:T(8,128)(2,1)S(1)}, u32[]{:S(2)}, u32[]{:S(2)}) collective-permute-start(bf16[1,32,2048]{2,1,0:T(8,128)(2,1)S(1)} %select_select_fusion.2), channel_id=1, source_target_pairs={{0,16},{1,17},{2,18},{3,19},{4,20},{5,21},{6,22},{7,23},{8,24},{9,... | collective-permute-start | bytes 393224 | tf_op jit(solution)/shard_map/while/body/eval_jaxpr/ppermute | solution.py:14
  178.8 8.3 %collective-permute-start = (bf16[1,32,2048]{2,1,0:T(8,128)(2,1)S(1)}, bf16[1,32,2048]{2,1,0:T(8,128)(2,1)S(1)}, u32[]{:S(2)}, u32[]{:S(2)}) collective-permute-start(bf16[1,32,2048]{2,1,0:T(8,128)(2,1)S(1)} %get-tuple-element.1319), channel_id=1, source_target_pairs={{0,16},{1,17},{2,18},{3,19},{4,20},{5,21},{6,22},{7,23},{8,24},{9,... | collective-permute-start | bytes 393224 | tf_op jit(solution)/shard_map/while/body/eval_jaxpr/ppermute | solution.py:14
  183.2 3.8 %collective-permute-start.1 = (bf16[1,32,2048]{2,1,0:T(8,128)(2,1)S(1)}, bf16[1,32,2048]{2,1,0:T(8,128)(2,1)S(1)}, u32[]{:S(2)}, u32[]{:S(2)}) collective-permute-start(bf16[1,32,2048]{2,1,0:T(8,128)(2,1)S(1)} %select_select_fusion.2), channel_id=1, source_target_pairs={{0,16},{1,17},{2,18},{3,19},{4,20},{5,21},{6,22},{7,23},{8,24},{9,... | collective-permute-start | bytes 393224 | tf_op jit(solution)/shard_map/while/body/eval_jaxpr/ppermute | solution.py:14
  188.2 16.5 %collective-permute-start = (bf16[1,32,2048]{2,1,0:T(8,128)(2,1)S(1)}, bf16[1,32,2048]{2,1,0:T(8,128)(2,1)S(1)}, u32[]{:S(2)}, u32[]{:S(2)}) collective-permute-start(bf16[1,32,2048]{2,1,0:T(8,128)(2,1)S(1)} %get-tuple-element.1319), channel_id=1, source_target_pairs={{0,16},{1,17},{2,18},{3,19},{4,20},{5,21},{6,22},{7,23},{8,24},{9,... | collective-permute-start | bytes 393224 | tf_op jit(solution)/shard_map/while/body/eval_jaxpr/ppermute | solution.py:14
  200.8 3.8 %collective-permute-start.1 = (bf16[1,32,2048]{2,1,0:T(8,128)(2,1)S(1)}, bf16[1,32,2048]{2,1,0:T(8,128)(2,1)S(1)}, u32[]{:S(2)}, u32[]{:S(2)}) collective-permute-start(bf16[1,32,2048]{2,1,0:T(8,128)(2,1)S(1)} %select_select_fusion.2), channel_id=1, source_target_pairs={{0,16},{1,17},{2,18},{3,19},{4,20},{5,21},{6,22},{7,23},{8,24},{9,... | collective-permute-start | bytes 393224 | tf_op jit(solution)/shard_map/while/body/eval_jaxpr/ppermute | solution.py:14
  205.0 22.1 %collective-permute-start.2 = (bf16[1,32,2048]{2,1,0:T(8,128)(2,1)S(1)}, bf16[1,32,2048]{2,1,0:T(8,128)(2,1)S(1)}, u32[]{:S(2)}, u32[]{:S(2)}) collective-permute-start(bf16[1,32,2048]{2,1,0:T(8,128)(2,1)S(1)} %get-tuple-element.1190), channel_id=1, source_target_pairs={{16,0},{17,1},{18,2},{19,3},{20,4},{21,5},{22,6},{23,7},{24,8},{25... | collective-permute-start | bytes 393224 | tf_op jit(solution)/shard_map/while/body/eval_jaxpr/ppermute | solution.py:14
  206.3 20.8 %collective-permute-start.3 = (bf16[1,32,2048]{2,1,0:T(8,128)(2,1)S(1)}, bf16[1,32,2048]{2,1,0:T(8,128)(2,1)S(1)}, u32[]{:S(2)}, u32[]{:S(2)}) collective-permute-start(bf16[1,32,2048]{2,1,0:T(8,128)(2,1)S(1)} %get-tuple-element.1191), channel_id=1, source_target_pairs={{16,0},{17,1},{18,2},{19,3},{20,4},{21,5},{22,6},{23,7},{24,8},{25... | collective-permute-start | bytes 393224 | tf_op jit(solution)/shard_map/while/body/eval_jaxpr/ppermute | solution.py:14
  227.1 5.4 %copy-start.2 = (bf16[1024,2048]{1,0:T(8,128)(2,1)S(1)}, bf16[1024,2048]{1,0:T(8,128)(2,1)}, u32[]{:S(2)}) copy-start(bf16[1024,2048]{1,0:T(8,128)(2,1)} %get-tuple-element.750) | copy-start | bytes 12582916 | tf_op jit(solution)/shard_map/while/body/eval_jaxpr/cond
  231.5 3.6 copy-start.1
  236.9 20.5 %collective-permute-start.2 = (bf16[1,32,2048]{2,1,0:T(8,128)(2,1)S(1)}, bf16[1,32,2048]{2,1,0:T(8,128)(2,1)S(1)}, u32[]{:S(2)}, u32[]{:S(2)}) collective-permute-start(bf16[1,32,2048]{2,1,0:T(8,128)(2,1)S(1)} %get-tuple-element.1190), channel_id=1, source_target_pairs={{16,0},{17,1},{18,2},{19,3},{20,4},{21,5},{22,6},{23,7},{24,8},{25... | collective-permute-start | bytes 393224 | tf_op jit(solution)/shard_map/while/body/eval_jaxpr/ppermute | solution.py:14
  238.2 19.3 %collective-permute-start.3 = (bf16[1,32,2048]{2,1,0:T(8,128)(2,1)S(1)}, bf16[1,32,2048]{2,1,0:T(8,128)(2,1)S(1)}, u32[]{:S(2)}, u32[]{:S(2)}) collective-permute-start(bf16[1,32,2048]{2,1,0:T(8,128)(2,1)S(1)} %get-tuple-element.1191), channel_id=1, source_target_pairs={{16,0},{17,1},{18,2},{19,3},{20,4},{21,5},{22,6},{23,7},{24,8},{25... | collective-permute-start | bytes 393224 | tf_op jit(solution)/shard_map/while/body/eval_jaxpr/ppermute | solution.py:14
  257.6 5.4 %copy-start.2 = (bf16[1024,2048]{1,0:T(8,128)(2,1)S(1)}, bf16[1024,2048]{1,0:T(8,128)(2,1)}, u32[]{:S(2)}) copy-start(bf16[1024,2048]{1,0:T(8,128)(2,1)} %get-tuple-element.750) | copy-start | bytes 12582916 | tf_op jit(solution)/shard_map/while/body/eval_jaxpr/cond
  261.9 3.1 copy-start.3
  261.9 3.6 copy-start.1
  267.4 21.9 %collective-permute-start.2 = (bf16[1,32,2048]{2,1,0:T(8,128)(2,1)S(1)}, bf16[1,32,2048]{2,1,0:T(8,128)(2,1)S(1)}, u32[]{:S(2)}, u32[]{:S(2)}) collective-permute-start(bf16[1,32,2048]{2,1,0:T(8,128)(2,1)S(1)} %get-tuple-element.1190), channel_id=1, source_target_pairs={{16,0},{17,1},{18,2},{19,3},{20,4},{21,5},{22,6},{23,7},{24,8},{25... | collective-permute-start | bytes 393224 | tf_op jit(solution)/shard_map/while/body/eval_jaxpr/ppermute | solution.py:14
  268.7 20.6 %collective-permute-start.3 = (bf16[1,32,2048]{2,1,0:T(8,128)(2,1)S(1)}, bf16[1,32,2048]{2,1,0:T(8,128)(2,1)S(1)}, u32[]{:S(2)}, u32[]{:S(2)}) collective-permute-start(bf16[1,32,2048]{2,1,0:T(8,128)(2,1)S(1)} %get-tuple-element.1191), channel_id=1, source_target_pairs={{16,0},{17,1},{18,2},{19,3},{20,4},{21,5},{22,6},{23,7},{24,8},{25... | collective-permute-start | bytes 393224 | tf_op jit(solution)/shard_map/while/body/eval_jaxpr/ppermute | solution.py:14
  289.4 5.4 %copy-start.2 = (bf16[1024,2048]{1,0:T(8,128)(2,1)S(1)}, bf16[1024,2048]{1,0:T(8,128)(2,1)}, u32[]{:S(2)}) copy-start(bf16[1024,2048]{1,0:T(8,128)(2,1)} %get-tuple-element.750) | copy-start | bytes 12582916 | tf_op jit(solution)/shard_map/while/body/eval_jaxpr/cond
  293.7 3.6 copy-start.1
  299.2 20.5 %collective-permute-start.2 = (bf16[1,32,2048]{2,1,0:T(8,128)(2,1)S(1)}, bf16[1,32,2048]{2,1,0:T(8,128)(2,1)S(1)}, u32[]{:S(2)}, u32[]{:S(2)}) collective-permute-start(bf16[1,32,2048]{2,1,0:T(8,128)(2,1)S(1)} %get-tuple-element.1190), channel_id=1, source_target_pairs={{16,0},{17,1},{18,2},{19,3},{20,4},{21,5},{22,6},{23,7},{24,8},{25... | collective-permute-start | bytes 393224 | tf_op jit(solution)/shard_map/while/body/eval_jaxpr/ppermute | solution.py:14
  300.5 19.3 %collective-permute-start.3 = (bf16[1,32,2048]{2,1,0:T(8,128)(2,1)S(1)}, bf16[1,32,2048]{2,1,0:T(8,128)(2,1)S(1)}, u32[]{:S(2)}, u32[]{:S(2)}) collective-permute-start(bf16[1,32,2048]{2,1,0:T(8,128)(2,1)S(1)} %get-tuple-element.1191), channel_id=1, source_target_pairs={{16,0},{17,1},{18,2},{19,3},{20,4},{21,5},{22,6},{23,7},{24,8},{25... | collective-permute-start | bytes 393224 | tf_op jit(solution)/shard_map/while/body/eval_jaxpr/ppermute | solution.py:14
  319.8 5.4 %copy-start.2 = (bf16[1024,2048]{1,0:T(8,128)(2,1)S(1)}, bf16[1024,2048]{1,0:T(8,128)(2,1)}, u32[]{:S(2)}) copy-start(bf16[1024,2048]{1,0:T(8,128)(2,1)} %get-tuple-element.750) | copy-start | bytes 12582916 | tf_op jit(solution)/shard_map/while/body/eval_jaxpr/cond
  324.2 3.6 copy-start.1
  329.7 21.9 %collective-permute-start.2 = (bf16[1,32,2048]{2,1,0:T(8,128)(2,1)S(1)}, bf16[1,32,2048]{2,1,0:T(8,128)(2,1)S(1)}, u32[]{:S(2)}, u32[]{:S(2)}) collective-permute-start(bf16[1,32,2048]{2,1,0:T(8,128)(2,1)S(1)} %get-tuple-element.1190), channel_id=1, source_target_pairs={{16,0},{17,1},{18,2},{19,3},{20,4},{21,5},{22,6},{23,7},{24,8},{25... | collective-permute-start | bytes 393224 | tf_op jit(solution)/shard_map/while/body/eval_jaxpr/ppermute | solution.py:14
  331.0 20.6 %collective-permute-start.3 = (bf16[1,32,2048]{2,1,0:T(8,128)(2,1)S(1)}, bf16[1,32,2048]{2,1,0:T(8,128)(2,1)S(1)}, u32[]{:S(2)}, u32[]{:S(2)}) collective-permute-start(bf16[1,32,2048]{2,1,0:T(8,128)(2,1)S(1)} %get-tuple-element.1191), channel_id=1, source_target_pairs={{16,0},{17,1},{18,2},{19,3},{20,4},{21,5},{22,6},{23,7},{24,8},{25... | collective-permute-start | bytes 393224 | tf_op jit(solution)/shard_map/while/body/eval_jaxpr/ppermute | solution.py:14
  (6 other events, 13.3 us)
Sparse Core Ops, SparseCore 0:
  10.2 53.2 all-gather.6
  65.6 49.0 all-gather.8
